TPU v7x, 32 devices: a whole 2x2x4 slice. The times are simulated.
32 devices in a mesh: groups: 2 (over y), events: 8 (over z, x), heads: 2 (over core).
Axes of the slice: x: 2, y: 2, z: 4, core: 2. Of those that a mesh axis runs over, the one named last changes fastest.
Arguments:
- inputs: bfloat16 [256, 1024], P(('groups', 'events')), parts along dimension 0, may hold values from -6 to 6
- cand_user: int32 [256], P('groups'), parts along dimension 0, may hold values from 0 to 3, as said below
- event_user: int32 [8192], P(('groups', 'events')), parts along dimension 0, may hold values from 0 to 3, as said below
- event_count: int32 [16], P(('groups', 'events')), parts along dimension 0, may hold values from 128 to 512, as said below
- w_qu: bfloat16 [1024, 2, 1024], P(None, None, 'heads'), may hold values from -0.1875 to 0.1875
- keys: bfloat16 [8192, 1024], P(('groups', 'events'), 'heads'), parts along dimension 0, may hold values from -6 to 6
- values: bfloat16 [8192, 1024], P(('groups', 'events'), 'heads'), parts along dimension 0, may hold values from -6 to 6
- gain: float32 [1024], P('heads'), may hold values from 0.1 to 1.9
- w_out: bfloat16 [1024, 1024], P('heads'), may hold values from -0.1875 to 0.1875
Outputs:
- scored: bfloat16 [256, 1024], P(('groups', 'events')), parts along dimension 0
There are 2 independent parts, one for each index of `groups`. A program takes and returns all parts, laid end to end along the dimension named above; an argument that names none is the same for every part. Nothing has to cross between parts.
Inputs may be any that keep to these rules, and one draw needn't show every extreme that they name: `event_count`: each cache shard's filled slots come first; some shard is full and some holds 128. `event_user`: Users' events are consecutive and in increasing user order over the whole cache; every user has 1 to 2047 events, and some user has exactly 2047. `cand_user`: every candidate belongs to a user that has at least one filled slot somewhere in the cache.
All inputs are finite; a program needn't handle non-finite values.
Results may differ from a plain program's by a relative error of at most 0.0075.
Values may be sent and summed in bfloat16 or wider, within the bound.
No kernel may reach another device: no remote copies, remote signals or barrier semaphores. Data moves between devices by JAX's collectives and lax.ppermute only.
A program may use at most 64 MiB of HBM per device.

v0:
```python
import math
import jax
import jax.numpy as jnp
from jax import lax
from jax.sharding import PartitionSpec as P

DH = 128
HD = 1024
epsilon = 1e-05


def shards(inputs, cand_user, event_user, event_count, w_qu, keys, values, gain, w_out):
    row_count = inputs.shape[0]
    feat_width = inputs.shape[1]
    local_width = w_qu.shape[2]
    heads_here = local_width // DH
    slot_total = keys.shape[0]
    score_scale = 1.0 / math.sqrt(DH)
    packed_weight = w_qu.reshape(feat_width, 2 * local_width)
    query_weight = packed_weight[:, :local_width]
    gate_weight = packed_weight[:, local_width:]
    gate_values = jax.nn.silu(
        jnp.dot(inputs, gate_weight, preferred_element_type=jnp.float32)
    ).astype(jnp.bfloat16)
    gathered_rows = lax.all_gather(inputs, "events", axis=0, tiled=True)
    queries = jax.nn.silu(
        jnp.dot(gathered_rows, query_weight, preferred_element_type=jnp.float32)
    ).astype(jnp.bfloat16)
    slot_index = jnp.arange(slot_total, dtype=jnp.int32)
    slot_valid = slot_index < event_count[0]
    key_heads = keys.reshape(slot_total, heads_here, DH)
    value_heads = values.reshape(slot_total, heads_here, DH)

    def attend_rows(query_rows, row_users):
        rows_here = query_rows.shape[0]
        query_block = query_rows.reshape(rows_here, heads_here, DH)
        user_match = ((row_users[:, None] == event_user[None, :]) & slot_valid[None, :]).astype(
            jnp.float32
        )
        scores = (
            jnp.einsum("chd,ehd->hce", query_block, key_heads, preferred_element_type=jnp.float32)
            * score_scale
        )
        attn_weights = (jax.nn.silu(scores) * user_match[None]).astype(jnp.bfloat16)
        partial_out = jnp.einsum(
            "hce,ehd->chd", attn_weights, value_heads, preferred_element_type=jnp.float32
        )
        return partial_out.reshape(rows_here, local_width)

    block_rows = math.gcd(row_count * lax.axis_size("events"), 512)
    block_count = row_count * lax.axis_size("events") // block_rows

    def compute_block(which_block):
        block_start = which_block * block_rows
        query_rows = lax.dynamic_slice_in_dim(queries, block_start, block_rows, 0)
        block_users = lax.dynamic_slice_in_dim(cand_user, block_start, block_rows, 0)
        return attend_rows(query_rows, block_users)

    stacked = lax.map(compute_block, jnp.arange(block_count, dtype=jnp.int32))
    attended = lax.psum_scatter(
        stacked.reshape(row_count * lax.axis_size("events"), local_width),
        "events",
        scatter_dimension=0,
        tiled=True,
    )
    first_moment = jnp.sum(attended, axis=1)
    second_moment = jnp.sum(attended * attended, axis=1)
    total_first, total_second = lax.psum((first_moment, second_moment), "heads")
    average = total_first / HD
    variance = total_second / HD - average * average
    normed = (attended - average[:, None]) * lax.rsqrt(variance + epsilon)[:, None] * gain
    gated = (normed * gate_values.astype(jnp.float32)).astype(jnp.bfloat16)
    projected = jnp.dot(gated, w_out, preferred_element_type=jnp.float32)
    summed_heads = lax.psum(projected, "heads")
    return (inputs.astype(jnp.float32) + summed_heads).astype(jnp.bfloat16)


def solution(mesh):
    placed = (
        P(("groups", "events"), None),
        P("groups"),
        P(("groups", "events")),
        P(("groups", "events")),
        P(None, None, "heads"),
        P(("groups", "events"), "heads"),
        P(("groups", "events"), "heads"),
        P("heads"),
        P("heads", None),
    )
    return jax.shard_map(
        shards, mesh=mesh, in_specs=placed, out_specs=P(("groups", "events"), None), check_vma=False
    )
```

profile of v0, /device:TPU:0, one launch (start us, length us, event | category | flops | bytes accessed | tf_op | source)
XLA Modules:
  0.0 143.9 jit_solution(11439747766623471906)
XLA Ops:
  6.5 0.0 copy-start
  6.5 0.0 reduce-scatter.2.cloned.1.call-start
  7.3 32.8 %all_gather.3 = bf16[128,1024]{1,0:T(8,128)(2,1)S(1)} all-gather(bf16[16,1024]{1,0:T(8,128)(2,1)} %param.9), channel_id=1, replica_groups=mesh['groups'=2,'events'=8,'heads'=2] {'events'}, dimensions={0}, use_global_device_ids=true | all-gather | bytes 294912 | tf_op jit(solution)/shard_map/all_gather | solution.py:25
  40.1 2.0 %copy.14 = bf16[512,512]{0,1:T(8,128)(2,1)} copy(bf16[512,512]{1,0:T(8,128)(2,1)} %param.15) | data formatting | bytes 1048576 | tf_op jit(solution)/shard_map/reshape | solution.py:32
  42.1 2.2 %copy.17 = bf16[128,8,2,512]{3,1,2,0:T(8,128)(2,1)S(1)} copy(bf16[128,8,2,512]{3,2,1,0:T(2,128)(2,1)} %bitcast.29) | data formatting | bytes 4194304
  44.3 0.0 copy-start.2
  44.3 0.0 copy-start.4
  44.3 1.0 fusion.14
  45.3 0.0 copy-done.2
  45.3 0.0 copy-done.4
  45.3 0.1 and_convert_fusion
  45.4 0.0 copy-start.1
  45.4 0.0 copy-start.3
  45.4 2.6 %fusion.4 = f32[4,128,128]{1,2,0:T(8,128)} fusion(bf16[512,4,128]{0,2,1:T(8,128)(2,1)} %bitcast.30, f32[128,512]{1,0:T(8,128)S(1)} %and_convert_fusion, bf16[16,4,8,128]{3,2,1,0:T(8,128)(2,1)} %fusion.14, bf16[512,512]{1,0:T(8,128)(2,1)} %param.14), kind=kOutput, calls=%fused_computation.6 | convolution fusion | flops 136052736 | bytes 1703936 | tf_op jit(solution)/shard_map/while/body/eval_jaxpr/hce,ehd->chd/dot_general | solution.py:45
  48.1 1.8 %copy.13 = f32[128,512]{1,0:T(8,128)} copy(f32[128,512]{0,1:T(8,128)} %bitcast.31) | data formatting | bytes 524288 | tf_op jit(solution)/shard_map/reshape | solution.py:61
  49.9 0.0 reduce-scatter.2.cloned.1.call-update
  49.9 0.0 all-reduce.3.cloned.1.call-start
  49.9 63.5 %reduce-scatter.2.cloned.1.call-done = f32[16,512]{1,0:T(8,128)} async-done(((f32[128,512]{1,0:T(8,128)}), f32[16,512]{1,0:T(8,128)}) %reduce-scatter.2.cloned.1.call-update) | async-done | bytes 32784 | tf_op jit(solution)/shard_map/reduce_scatter | solution.py:60
  113.5 0.9 fusion.38
  114.3 2.5 %all-reduce = (f32[16]{0:T(128)S(1)}, f32[16]{0:T(128)S(1)}) all-reduce(f32[16]{0:T(128)S(1)} %get-tuple-element.20, f32[16]{0:T(128)S(1)} %get-tuple-element.19), channel_id=1, replica_groups=mesh['groups'=2,'events'=8,'heads'=2] {'heads'}, use_global_device_ids=true, to_apply=%region_4.5 | all-reduce | flops 32 | bytes 256 | tf_op jit(solution)/shard_map/psum | solution.py:68
  116.8 0.0 copy-done
  116.8 0.0 copy-done.1
  116.8 0.0 copy-done.3
  116.8 1.9 %fusion.26 = f32[16,1024]{1,0:T(8,128)} fusion(bf16[512,1024]{1,0:T(8,128)(2,1)S(1)} %copy-done, bf16[16,1024]{1,0:T(8,128)(2,1)S(1)} %copy-done.1, bf16[1024,1024]{1,0:T(8,128)(2,1)S(1)} %bitcast.28, f32[16,512]{1,0:T(8,128)} %reduce-scatter.2.cloned.1.call-done, f32[512]{0:T(512)S(1)} %copy-done.3, f32[16]{0:T(128)S(1)} %get-tuple-element.32, ...), kind=kOutput, calls=%fused_computation.20 | convolution fusion | flops 33644544 | bytes 2231296 | tf_op jit(solution)/shard_map/dot_general | solution.py:73
  118.7 0.0 all-reduce.3.cloned.1.call-update
  118.7 16.9 %all-reduce.3.cloned.1.call-done = f32[16,1024]{1,0:T(8,128)} async-done(((f32[16,1024]{1,0:T(8,128)}), f32[16,1024]{1,0:T(8,128)}) %all-reduce.3.cloned.1.call-update) | async-done | bytes 65552 | tf_op jit(solution)/shard_map/psum | solution.py:74
  135.6 1.5 %add_convert_fusion = bf16[16,1024]{1,0:T(8,128)(2,1)} fusion(f32[16,1024]{1,0:T(8,128)} %all-reduce.3.cloned.1.call-done, bf16[16,1024]{1,0:T(8,128)(2,1)S(1)} %copy-done.1), kind=kLoop, calls=%fused_computation.17 | loop fusion | flops 49152 | bytes 131072 | tf_op jit(solution)/shard_map/convert_element_type | solution.py:75
  (2 shorter events, 0.0 us)
Async XLA Ops:
  6.5 110.3 %copy-start = (bf16[512,1024]{1,0:T(8,128)(2,1)S(1)}, bf16[512,1024]{1,0:T(8,128)(2,1)}, u32[]{:S(2)}) copy-start(bf16[512,1024]{1,0:T(8,128)(2,1)} %param.17) | copy-start | bytes 3145732
  6.5 106.9 %reduce-scatter.2.cloned.1.call-start = ((), (), s32[]{:S(2)}) async-start(), calls=%async_computation.1 | async-start | bytes 294912 | tf_op jit(solution)/shard_map/reduce_scatter | solution.py:60
  44.3 1.0 copy-start.2
  44.3 1.0 copy-start.4
  45.4 71.4 %copy-start.1 = (bf16[16,1024]{1,0:T(8,128)(2,1)S(1)}, bf16[16,1024]{1,0:T(8,128)(2,1)}, u32[]{:S(2)}) copy-start(bf16[16,1024]{1,0:T(8,128)(2,1)} %param.9) | copy-start | bytes 98308
  45.4 71.4 %copy-start.3 = (f32[512]{0:T(512)S(1)}, f32[512]{0:T(512)}, u32[]{:S(2)}) copy-start(f32[512]{0:T(512)} %param.16) | copy-start | bytes 6148
  49.9 85.7 %all-reduce.3.cloned.1.call-start = ((), (), s32[]{:S(2)}) async-start(), calls=%async_computation.2 | async-start | bytes 131072 | tf_op jit(solution)/shard_map/psum | solution.py:74
Sparse Core Ops, SparseCore 0:
  50.0 63.4 reduce-scatter.1
  118.8 16.7 all-reduce.2
where the time goes:
time: 144 us
  waiting for transfers between devices  80.5 us (56%)
  blocking collectives  35.2 us (24%)
  between operations  14.2 us (10%)
  local copies, waits for them, and re-layouts  6 us (4%)
  matrix products  5.52 us (4%)
  other arithmetic  2.45 us (2%)
    reduce_scatter x1, waiting for transfers between devices, shards(): lax.psum_scatter(stacked.reshape(row_count * lax.axis_size('events'), loc...  63.5 us
    all_gather x1, blocking collectives, shards(): gathered_rows = lax.all_gather(inputs, 'events', axis=0, tiled=True)  32.8 us
    psum x1, waiting for transfers between devices, shards(): summed_heads = lax.psum(projected, 'heads')  16.9 us
  transfers between devices with their start and end apart: 2, of which 2 were waited for; matrix products, arithmetic and copies ran while one was open for 0% of the time, Pallas kernels for 0%

commit v1 on v0

--- a/solution.py
+++ b/solution.py
@@ -71,7 +71,7 @@
     normed = (attended - average[:, None]) * lax.rsqrt(variance + epsilon)[:, None] * gain
     gated = (normed * gate_values.astype(jnp.float32)).astype(jnp.bfloat16)
     projected = jnp.dot(gated, w_out, preferred_element_type=jnp.float32)
-    summed_heads = lax.psum(projected, "heads")
+    summed_heads = jnp.sum(lax.all_gather(projected, axis_name="heads"), axis=0)
     return (inputs.astype(jnp.float32) + summed_heads).astype(jnp.bfloat16)
 
 

time: 144 us -> 128 us (0.89)
  waiting for transfers between devices: 80.5 us -> 63.6 us
  blocking collectives: 35.2 us -> 37.1 us
    psum x1 -> x0, waiting for transfers between devices: 16.9 us -> none  [shards(): summed_heads = lax.psum(projected, 'heads')]
    all_gather x0 -> x1, blocking collectives: none -> 1.9 us  [shards(): summed_heads = jnp.sum(lax.all_gather(projected, axis_name='heads'), axis=0)]
  transfers between devices with their start and end apart: 2 -> 1, of which waited for: 2 -> 1; matrix products, arithmetic and copies ran while one was open for 0% -> 0% of each run, Pallas kernels for 0% -> 0%
where the time goes in v1:
time: 128 us; the launch traced here: 127 us
  waiting for transfers between devices  63.6 us (50%)
  blocking collectives  37.1 us (29%)
  between operations  14.2 us (11%)
  local copies, waits for them, and re-layouts  6 us (5%)
  matrix products  4.89 us (4%)
  other arithmetic  1.63 us (1%)
    reduce_scatter x1, waiting for transfers between devices, shards(): lax.psum_scatter(stacked.reshape(row_count * lax.axis_size('events'), loc...  63.6 us
    all_gather x1, blocking collectives, shards(): gathered_rows = lax.all_gather(inputs, 'events', axis=0, tiled=True)  32.8 us
    dot_general x1, matrix products, attend_rows(): jnp.einsum('hce,ehd->chd', attn_weights, value_heads, preferred_element_t...  2.65 us
  transfers between devices with their start and end apart: 1, of which 1 were waited for; matrix products, arithmetic and copies ran while one was open for 0% of the time, Pallas kernels for 0%

profile of v1, /device:TPU:0, one launch (start us, length us, event | category | flops | bytes accessed | tf_op | source)
XLA Modules:
  0.0 127.4 jit_solution(3170197751630035930)
XLA Ops:
  6.5 0.0 copy-start
  6.5 0.0 reduce-scatter.2.cloned.1.call-start
  7.3 32.8 %all_gather.9 = bf16[128,1024]{1,0:T(8,128)(2,1)S(1)} all-gather(bf16[16,1024]{1,0:T(8,128)(2,1)} %param.9), channel_id=1, replica_groups=mesh['groups'=2,'events'=8,'heads'=2] {'events'}, dimensions={0}, use_global_device_ids=true | all-gather | bytes 294912 | tf_op jit(solution)/shard_map/all_gather | solution.py:25
  40.1 2.0 %copy.14 = bf16[512,512]{0,1:T(8,128)(2,1)} copy(bf16[512,512]{1,0:T(8,128)(2,1)} %param.15) | data formatting | bytes 1048576 | tf_op jit(solution)/shard_map/reshape | solution.py:32
  42.1 2.2 %copy.17 = bf16[128,8,2,512]{3,1,2,0:T(8,128)(2,1)S(1)} copy(bf16[128,8,2,512]{3,2,1,0:T(2,128)(2,1)} %bitcast.30) | data formatting | bytes 4194304
  44.3 0.0 copy-start.2
  44.3 0.0 copy-start.4
  44.3 1.0 fusion.14
  45.3 0.0 copy-done.2
  45.3 0.0 copy-done.4
  45.3 0.1 and_convert_fusion
  45.4 0.0 copy-start.1
  45.4 0.0 copy-start.3
  45.4 2.6 %fusion.4 = f32[4,128,128]{1,2,0:T(8,128)} fusion(bf16[512,4,128]{0,2,1:T(8,128)(2,1)} %bitcast.32, f32[128,512]{1,0:T(8,128)S(1)} %and_convert_fusion, bf16[16,4,8,128]{3,2,1,0:T(8,128)(2,1)} %fusion.14, bf16[512,512]{1,0:T(8,128)(2,1)} %param.14), kind=kOutput, calls=%fused_computation.6 | convolution fusion | flops 136052736 | bytes 1703936 | tf_op jit(solution)/shard_map/while/body/eval_jaxpr/hce,ehd->chd/dot_general | solution.py:45
  48.1 1.8 %copy.13 = f32[128,512]{1,0:T(8,128)} copy(f32[128,512]{0,1:T(8,128)} %bitcast.33) | data formatting | bytes 524288 | tf_op jit(solution)/shard_map/reshape | solution.py:61
  49.9 0.0 reduce-scatter.2.cloned.1.call-update
  49.9 63.6 %reduce-scatter.2.cloned.1.call-done = f32[16,512]{1,0:T(8,128)} async-done(((f32[128,512]{1,0:T(8,128)}), f32[16,512]{1,0:T(8,128)}) %reduce-scatter.2.cloned.1.call-update) | async-done | bytes 32784 | tf_op jit(solution)/shard_map/reduce_scatter | solution.py:60
  113.5 0.9 fusion.38
  114.3 2.5 %all-reduce = (f32[16]{0:T(128)S(1)}, f32[16]{0:T(128)S(1)}) all-reduce(f32[16]{0:T(128)S(1)} %get-tuple-element.20, f32[16]{0:T(128)S(1)} %get-tuple-element.19), channel_id=1, replica_groups=mesh['groups'=2,'events'=8,'heads'=2] {'heads'}, use_global_device_ids=true, to_apply=%region_4.5 | all-reduce | flops 32 | bytes 256 | tf_op jit(solution)/shard_map/psum | solution.py:68
  116.8 0.0 copy-done
  116.8 0.0 copy-done.1
  116.8 0.0 copy-done.3
  116.8 1.2 fusion.26
  118.1 1.9 %all-gather = f32[32,1024]{1,0:T(8,128)S(1)} all-gather(f32[16,1024]{1,0:T(8,128)S(1)} %fusion.26), channel_id=2, replica_groups=mesh['groups'=2,'events'=8,'heads'=2] {'heads'}, dimensions={0}, use_global_device_ids=true | all-gather | bytes 196608 | tf_op jit(solution)/shard_map/all_gather | solution.py:74
  120.0 0.6 add_convert_fusion
  (3 shorter events, 0.0 us)
Async XLA Ops:
  6.5 110.3 %copy-start = (bf16[512,1024]{1,0:T(8,128)(2,1)S(1)}, bf16[512,1024]{1,0:T(8,128)(2,1)}, u32[]{:S(2)}) copy-start(bf16[512,1024]{1,0:T(8,128)(2,1)} %param.17) | copy-start | bytes 3145732
  6.5 106.9 %reduce-scatter.2.cloned.1.call-start = ((), (), s32[]{:S(2)}) async-start(), calls=%async_computation.1 | async-start | bytes 294912 | tf_op jit(solution)/shard_map/reduce_scatter | solution.py:60
  44.3 1.0 copy-start.2
  44.3 1.0 copy-start.4
  45.4 71.4 %copy-start.1 = (bf16[16,1024]{1,0:T(8,128)(2,1)S(1)}, bf16[16,1024]{1,0:T(8,128)(2,1)}, u32[]{:S(2)}) copy-start(bf16[16,1024]{1,0:T(8,128)(2,1)} %param.9) | copy-start | bytes 98308
  45.4 71.4 %copy-start.3 = (f32[512]{0:T(512)S(1)}, f32[512]{0:T(512)}, u32[]{:S(2)}) copy-start(f32[512]{0:T(512)} %param.16) | copy-start | bytes 6148
Sparse Core Ops, SparseCore 0:
  50.0 63.4 reduce-scatter.1
